TPU v7x, 256 devices: a whole 4x4x8 slice. The times are simulated.
256 devices in a mesh: segment: 4 (over y), ctx: 32 (over x_hi, z, core), tp: 2 (over x_lo).
Axes of the slice: x: 4 (x_hi: 2, x_lo: 2; x = x_hi * 2 + x_lo), y: 4, z: 8, core: 2. Of those that a mesh axis runs over, the one named last changes fastest.
Arguments:
- held: bfloat16 [4, 8192, 3584], P('segment', 'ctx'), may hold values from -6 to 6
- text: bfloat16 [8192, 3584], P('ctx'), may hold values from -6 to 6
- frames: bfloat16 [4096, 1024], P('ctx'), may hold values from -6 to 6
- join: int32 [64], P('ctx'), may hold values from 0 to 8128, as said below
- ln_gain: float32 [1024], replicated, may hold values from 0.1 to 1.9
- w_proj: bfloat16 [1024, 3584], P('tp'), may hold values from -0.1875 to 0.1875
- b_proj: float32 [3584], replicated, may hold values from -3 to 3
- norm_gain: float32 [3, 3584], replicated, may hold values from 0.1 to 1.9
- w_qkv: bfloat16 [3, 3584, 2304], P(None, 'ctx', 'tp'), may hold values from -0.09375 to 0.09375
- b_qkv: float32 [3, 2304], P(None, 'tp'), may hold values from -4 to 4
- w_out: bfloat16 [3, 1792, 3584], P(None, 'tp', 'ctx'), may hold values from -1.5 to 1.5
Outputs:
- segment_out: bfloat16 [4, 8192, 3584], P('segment', 'ctx')
Inputs may be any that keep to these rules, and one draw needn't show every extreme that they name: `join`: frames never intersect; the 2 frames f with f // 2 == d lie in order inside positions d * 256 to (d + 1) * 256 - 1.
All inputs are finite; a program needn't handle non-finite values.
Results may differ from a plain program's by a relative error of at most 0.015.
Values may be sent and summed in bfloat16 or wider, within the bound.
No kernel may reach another device: no remote copies, remote signals or barrier semaphores. Data moves between devices by JAX's collectives and lax.ppermute only.
A program may use at most 128 MiB of HBM per device.

v0:
```python
from functools import partial
import jax
import jax.numpy as jnp
from jax import lax
from jax.sharding import PartitionSpec as P

HD = 128
GROUP = 7
FRAME = 64


def shifted(value, axis, by):
    devices = lax.axis_size(axis)
    pairs = [(i, i + by) for i in range(devices) if 0 <= i + by < devices]
    return lax.ppermute(value, axis, pairs)


def update_state(softmax_state, query_flat, query_pos, keys_in, values_in, offset):
    peak_old, total_old, accum_old = softmax_state
    key_pos = jnp.arange(keys_in.shape[0], dtype=jnp.int32)
    scores = jnp.dot(query_flat, keys_in.T, preferred_element_type=jnp.float32) * HD ** (-0.5)
    allowed = key_pos[None, :] <= query_pos[:, None]
    scores = jnp.where(allowed, scores, -1e30)
    peak_new = jnp.maximum(peak_old, jnp.max(scores, axis=1))
    weights = jnp.where(allowed, jnp.exp(scores - peak_new[:, None]), 0.0)
    total_new = jnp.sum(weights, axis=1)
    accum_new = jnp.dot(weights.astype(jnp.bfloat16), values_in, preferred_element_type=jnp.float32)
    return (peak_new, total_new, accum_new)


def keep_state(softmax_state):
    return softmax_state


def on_device(held, text, frames, join, ln_gain, w_proj, b_proj, norm_gain, w_qkv, b_qkv, w_out):
    segment_id = lax.axis_index("segment")
    ctx_id = lax.axis_index("ctx")
    tp_id = lax.axis_index("tp")
    hidden_in = shifted(held[0], "segment", 1)
    tok_rows = hidden_in.shape[0]
    half_rows = tok_rows // 2
    layer_id = jnp.maximum(segment_id - 1, 0)
    weight_qkv = lax.dynamic_index_in_dim(w_qkv, layer_id, 0, keepdims=False)
    bias_qkv = lax.dynamic_index_in_dim(b_qkv, layer_id, 0, keepdims=False)
    layer_gain = lax.dynamic_index_in_dim(norm_gain, layer_id, 0, keepdims=False)
    weight_out = lax.dynamic_index_in_dim(w_out, layer_id, 0, keepdims=False)
    inputs = hidden_in.astype(jnp.float32)
    normed = (
        inputs * lax.rsqrt(jnp.mean(inputs * inputs, axis=1, keepdims=True) + 1e-06) * layer_gain
    ).astype(jnp.bfloat16)
    merged = jnp.dot(
        normed,
        lax.all_gather(weight_qkv, "ctx", axis=0, tiled=True),
        preferred_element_type=jnp.float32,
    )
    merged = (merged + bias_qkv).astype(jnp.bfloat16)
    query_cols = GROUP * HD
    queries = merged[:, :query_cols]
    local_steps = jnp.arange(half_rows, dtype=jnp.int32)
    first_pos = ctx_id * tok_rows + local_steps
    second_q = queries[half_rows:]
    second_pos = ctx_id * tok_rows + half_rows + local_steps
    first_flat = queries[:half_rows].reshape(half_rows * GROUP, HD)
    second_flat = second_q.reshape(half_rows * GROUP, HD)
    first_qpos = jnp.repeat(first_pos, GROUP)
    second_qpos = jnp.repeat(second_pos, GROUP)
    flat_rows = half_rows * GROUP
    empty = (
        jnp.full((flat_rows,), -1e30, jnp.float32),
        jnp.zeros((flat_rows,), jnp.float32),
        jnp.zeros((flat_rows, HD), jnp.float32),
    )
    carried = (empty, empty)
    offset = jnp.int32(0)
    kv_in = lax.all_gather(merged[:, query_cols : query_cols + 2 * HD], "ctx", axis=0, tiled=True)
    keys_in = kv_in[:, :HD]
    values_in = kv_in[:, HD:]
    updated = []
    for softmax_state, query_flat, query_pos in (
        (carried[0], first_flat, first_qpos),
        (carried[1], second_flat, second_qpos),
    ):
        step_fn = partial(
            update_state,
            query_flat=query_flat,
            query_pos=query_pos,
            keys_in=keys_in,
            values_in=values_in,
            offset=offset,
        )
        updated.append(lax.cond(offset <= jnp.max(query_pos), step_fn, keep_state, softmax_state))

    def finish(softmax_state):
        return (
            (softmax_state[2] / softmax_state[1][:, None])
            .astype(jnp.bfloat16)
            .reshape(half_rows, GROUP * HD)
        )

    first_out = finish(updated[0])
    second_out = finish(updated[1])
    attended = jnp.concatenate([first_out, second_out], axis=0)
    partial_model = jnp.dot(
        attended,
        lax.all_gather(weight_out, "ctx", axis=1, tiled=True),
        preferred_element_type=jnp.float32,
    )
    positions = ctx_id * tok_rows + jnp.arange(tok_rows, dtype=jnp.int32)[:, None]
    starts = join[None, :]
    inside = (positions >= starts) & (positions < starts + FRAME)
    frame_base = (jnp.arange(join.shape[0], dtype=jnp.int32) * FRAME)[None, :]
    source = jnp.sum(jnp.where(inside, frame_base + positions - starts, 0), axis=1)
    is_vision = jnp.any(inside, axis=1)

    def vision_term():
        frame_in = frames.astype(jnp.float32)
        center = jnp.mean(frame_in, axis=1, keepdims=True)
        spread = jnp.mean((frame_in - center) * (frame_in - center), axis=1, keepdims=True)
        normed_frames = ((frame_in - center) * lax.rsqrt(spread + 1e-06) * ln_gain).astype(
            jnp.bfloat16
        )
        vis_width = w_proj.shape[0]
        normed_half = lax.dynamic_slice_in_dim(normed_frames, tp_id * vis_width, vis_width, 1)
        projected = jnp.dot(normed_half, w_proj, preferred_element_type=jnp.float32)
        return jnp.where(is_vision[:, None], jnp.take(projected, source, axis=0), 0.0)

    def model_term():
        return partial_model

    is_first = segment_id == 0
    section_term = lax.cond(is_first, vision_term, model_term)
    baseline = jnp.where(
        is_first, jnp.where(is_vision[:, None], b_proj[None, :], text.astype(jnp.float32)), inputs
    )
    own_term = section_term.astype(jnp.bfloat16)
    other_term = lax.ppermute(own_term, "tp", [(0, 1), (1, 0)])
    summed = own_term.astype(jnp.float32) + other_term.astype(jnp.float32)
    result = (baseline + summed).astype(jnp.bfloat16)
    return result[None]


def solution(mesh):
    return jax.shard_map(
        on_device,
        mesh=mesh,
        in_specs=(
            P("segment", "ctx", None),
            P("ctx", None),
            P("ctx", None),
            P("ctx"),
            P(),
            P("tp", None),
            P(),
            P(),
            P(None, "ctx", "tp"),
            P(None, "tp"),
            P(None, "tp", "ctx"),
        ),
        out_specs=P("segment", "ctx", None),
        check_vma=False,
    )
```

profile of v0, /device:TPU:1, one launch (start us, length us, event | category | flops | bytes accessed | tf_op | source)
XLA Modules:
  0.0 367.7 jit_solution(14345656262956970861)
XLA Ops:
  6.5 1.1 copy-done
  7.7 0.7 constant_dynamic-slice_fusion.1
  8.5 4.1 %collective-permute-start = (bf16[256,3584]{1,0:T(8,128)(2,1)}, bf16[256,3584]{1,0:T(8,128)(2,1)S(1)}, u32[]{:S(2)}, u32[]{:S(2)}) collective-permute-start(bf16[256,3584]{1,0:T(8,128)(2,1)} %bitcast.20), channel_id=1, source_target_pairs={{0,64},{64,128},{128,192},{1,65},{65,129},{129,193},{2,66},{66,130... | collective-permute-start | bytes 5505032 | tf_op jit(solution)/shard_map/ppermute | solution.py:15
  12.6 0.7 dynamic-slice_reduce_fusion.1
  13.4 0.9 dynamic-slice_reduce_fusion
  14.2 37.2 %collective-permute-done = bf16[256,3584]{1,0:T(8,128)(2,1)S(1)} collective-permute-done((bf16[256,3584]{1,0:T(8,128)(2,1)}, bf16[256,3584]{1,0:T(8,128)(2,1)S(1)}, u32[]{:S(2)}, u32[]{:S(2)}) %collective-permute-start) | collective-permute-done | bytes 1835040 | tf_op jit(solution)/shard_map/ppermute | solution.py:15
  51.5 0.4 fusion.31
  51.9 63.3 %all-gather.8.cloned.1.call-done = bf16[1,3584,1152]{2,1,0:T(8,128)(2,1)} async-done(((bf16[1,112,1152]{2,1,0:T(8,128)(2,1)}), bf16[1,3584,1152]{2,1,0:T(8,128)(2,1)}) %all-gather.8.cloned.1.call-update) | async-done | bytes 8257552 | tf_op jit(solution)/shard_map/all_gather | solution.py:53
  115.3 6.8 %fusion.37 = bf16[256,1152]{1,0:T(8,128)(2,1)} fusion(bf16[1,3584,1152]{2,1,0:T(8,128)(2,1)} %all-gather.8.cloned.1.call-done, bf16[256,3584]{1,0:T(8,128)(2,1)S(1)} %collective-permute-done, f32[3584]{0:T(1024)S(1)} %dynamic-slice_reduce_fusion, f32[256]{0:T(256)S(1)} %add_rsqrt_fusion.1, f32[1152]{0:T(1024)S(1)} %dynamic-slice_reduce_fusion.1), kind=kOutput, calls=%fused_computation.56 | convolution fusion | flops 2118189056 | bytes 10702336 | tf_op jit(solution)/shard_map/dot_general | solution.py:51
  122.0 1.6 slice.25
  123.7 1.6 constant_dynamic-slice_fusion
  125.3 0.7 broadcast_reduce_fusion.1
  126.7 0.7 broadcast_reduce_fusion
  128.1 0.1 fusion.48
  128.3 78.7 %all-gather.6.cloned.1.call-done = bf16[8192,256]{1,0:T(8,128)(2,1)} async-done(((bf16[256,256]{1,0:T(8,128)(2,1)}), bf16[8192,256]{1,0:T(8,128)(2,1)}) %all-gather.6.cloned.1.call-update) | async-done | bytes 4194320 | tf_op jit(solution)/shard_map/all_gather | solution.py:75
  207.0 3.9 %fusion.49 = (bf16[8192,128]{1,0:T(8,128)(2,1)S(1)}, bf16[8192,128]{1,0:T(8,128)(2,1)}) fusion(bf16[8192,256]{1,0:T(8,128)(2,1)} %all-gather.6.cloned.1.call-done), kind=kLoop, calls=%fused_computation.79 | loop fusion | bytes 8388608 | tf_op jit(solution)/shard_map/slice | solution.py:77
  211.0 42.8 %conditional.3 = (f32[896]{0:T(1024)S(1)}, f32[896,128]{1,0:T(8,128)S(1)}) conditional(s32[]{:T(128)} %convert_element_type.60, () %tuple.37, (s32[128,7]{1,0:T(8,128)S(1)}, bf16[256,1152]{1,0:T(8,128)(2,1)}, bf16[8192,128]{1,0:T(8,128)(2,1)}, bf16[8192,128]{1,0:T(8,128)(2,1)S(1)}) %tuple.38), branch_computations={%region_3.4_spmd, %region_4.7_spmd} | conditional | flops 3875535872 | bytes 93919760 | solution.py:91
  211.0 0.2 le.30
  211.2 1.0 slice.15
  212.1 0.2 reshape.63
  212.4 13.8 %fusion = (f32[896]{0:T(1024)S(1)}, f32[896,8192]{1,0:T(8,128)}) fusion(s32[896]{0:T(1024)S(1)} %le.30, bf16[896,128]{1,0:T(8,128)(2,1)S(1)} %reshape.63, bf16[8192,128]{1,0:T(8,128)(2,1)} %get-tuple-element.49), kind=kOutput, calls=%fused_computation.4 | convolution fusion | flops 1908407424 | bytes 31693824 | tf_op jit(solution)/shard_map/cond/branch_1_fun/dot_general | solution.py:21
  226.2 13.1 %fusion.3 = f32[896,128]{1,0:T(8,128)S(1)} fusion(bf16[8192,128]{1,0:T(8,128)(2,1)S(1)} %get-tuple-element.50, f32[896,8192]{1,0:T(8,128)} %get-tuple-element.92, f32[896]{0:T(1024)S(1)} %broadcast_maximum_fusion, s32[896]{0:T(1024)S(1)} %le.30), kind=kOutput, calls=%fused_computation.7 | convolution fusion | flops 1923088384 | bytes 31923200 | tf_op jit(solution)/shard_map/cond/branch_1_fun/dot_general | solution.py:27
  239.3 14.4 %fusion.2 = f32[896]{0:T(1024)S(1)} fusion(f32[896,8192]{1,0:T(8,128)} %get-tuple-element.92, f32[896]{0:T(1024)S(1)} %broadcast_maximum_fusion, s32[896]{0:T(1024)S(1)} %le.30), kind=kLoop, calls=%fused_computation.6 | loop fusion | flops 44039296 | bytes 29370880 | tf_op jit(solution)/shard_map/cond/branch_1_fun/reduce_sum | solution.py:26
  253.7 0.2 divide_convert_fusion.1
  253.9 0.2 reshape.67
  254.2 0.1 broadcast_in_dim.105
  254.3 43.7 %conditional.4 = (f32[896]{0:T(1024)S(1)}, f32[896,128]{1,0:T(8,128)S(1)}) conditional(s32[]{:T(128)} %convert_element_type.64, () %tuple.39, (s32[128,7]{1,0:T(8,128)S(1)}, bf16[256,1152]{1,0:T(8,128)(2,1)}, bf16[8192,128]{1,0:T(8,128)(2,1)}, bf16[8192,128]{1,0:T(8,128)(2,1)S(1)}) %tuple.40), branch_computations={%region_8.9_spmd, %region_9.12_spmd} | conditional | flops 3875535872 | bytes 93919760 | solution.py:91
  254.5 0.2 le.38
  254.7 1.0 slice.16
  255.7 0.2 reshape.64
  255.9 14.2 %fusion.8 = (f32[896]{0:T(1024)S(1)}, f32[896,8192]{1,0:T(8,128)}) fusion(s32[896]{0:T(1024)S(1)} %le.38, bf16[896,128]{1,0:T(8,128)(2,1)S(1)} %reshape.64, bf16[8192,128]{1,0:T(8,128)(2,1)} %get-tuple-element.53), kind=kOutput, calls=%fused_computation.15 | convolution fusion | flops 1908407424 | bytes 31693824 | tf_op jit(solution)/shard_map/cond/branch_1_fun/dot_general | solution.py:21
  270.1 13.1 %fusion.11 = f32[896,128]{1,0:T(8,128)S(1)} fusion(bf16[8192,128]{1,0:T(8,128)(2,1)S(1)} %get-tuple-element.54, f32[896,8192]{1,0:T(8,128)} %get-tuple-element.94, f32[896]{0:T(1024)S(1)} %broadcast_maximum_fusion.1, s32[896]{0:T(1024)S(1)} %le.38), kind=kOutput, calls=%fused_computation.18 | convolution fusion | flops 1923088384 | bytes 31923200 | tf_op jit(solution)/shard_map/cond/branch_1_fun/dot_general | solution.py:27
  283.2 14.8 %fusion.10 = f32[896]{0:T(1024)S(1)} fusion(f32[896,8192]{1,0:T(8,128)} %get-tuple-element.94, f32[896]{0:T(1024)S(1)} %broadcast_maximum_fusion.1, s32[896]{0:T(1024)S(1)} %le.38), kind=kLoop, calls=%fused_computation.17 | loop fusion | flops 44039296 | bytes 29370880 | tf_op jit(solution)/shard_map/cond/branch_1_fun/reduce_sum | solution.py:26
  298.0 0.2 divide_convert_fusion
  298.2 0.2 reshape.68
  298.4 2.6 all-gather.10.cloned.1.call-done
  301.0 6.2 %fusion.27 = bf16[256,3584]{1,0:T(8,128)(2,1)} fusion(bf16[1,896,3584]{1,2,0:T(8,128)(2,1)} %all-gather.10.cloned.1.call-done, bf16[128,896]{1,0:T(8,128)(2,1)S(1)} %reshape.68, bf16[128,896]{1,0:T(8,128)(2,1)S(1)} %reshape.67), kind=kOutput, calls=%fused_computation.45 | convolution fusion | flops 1645084672 | bytes 8716288 | tf_op jit(solution)/shard_map/dot_general | solution.py:103
  307.2 7.3 %conditional.5 = (bf16[256,3584]{1,0:T(8,128)(2,1)}) conditional(s32[]{:T(128)} %convert_element_type.59, bf16[256,3584]{1,0:T(8,128)(2,1)} %fusion.27, (pred[256]{0:T(512)(128)(4,1)S(1)}, pred[256,2]{0,1:T(4,128)(4,1)S(1)}, bf16[128,1024]{1,0:T(8,128)(2,1)S(1)}, f32[1024]{0:T(1024)S(1)}, s32[]{:T(128)}, /*index=5*/bf16[512,3584]{1,0:T(8,128)(2,1)}, ...), branch_computations={%region_13.14_spmd, %region_14.17_spmd} | conditional | flops 472585344 | bytes 13264226 | solution.py:131
  307.2 0.1 dynamic-slice
  307.3 0.1 convert_reduce_fusion
  307.4 0.2 multiply_reduce_fusion
  307.6 2.7 fusion.18
  310.4 0.1 fusion.23
  310.5 1.7 gather_fusion
  312.2 2.2 select_select_fusion
  314.5 0.3 collective-permute-start.1
  314.8 41.2 %collective-permute-done.1 = bf16[256,3584]{1,0:T(8,128)(2,1)S(1)} collective-permute-done((bf16[256,3584]{1,0:T(8,128)(2,1)}, bf16[256,3584]{1,0:T(8,128)(2,1)S(1)}, u32[]{:S(2)}, u32[]{:S(2)}) %collective-permute-start.1) | collective-permute-done | bytes 1835040 | tf_op jit(solution)/shard_map/ppermute | solution.py:136
  356.0 5.1 %fusion.41 = bf16[1,256,3584]{2,1,0:T(8,128)(2,1)} fusion(bf16[256,3584]{1,0:T(8,128)(2,1)S(1)} %collective-permute-done.1, bf16[256,3584]{1,0:T(8,128)(2,1)} %get-tuple-element.107, bf16[256,3584]{1,0:T(8,128)(2,1)} %copy-done.2, bf16[256,3584]{1,0:T(8,128)(2,1)} %param.18, f32[3584]{0:T(1024)S(1)} %copy-done.4, pred[256]{0:T(512)(128)(4,1)S(1)} %get-tuple-element.89, ...), kind=kLoop, calls=%fused_computation.57 | loop fusion | flops 8257536 | bytes 9189633 | tf_op jit(solution)/shard_map/broadcast_in_dim | solution.py:139
  (36 shorter events, 0.4 us)
Async XLA Ops:
  6.5 1.1 copy-start
  6.5 108.7 %all-gather.8.cloned.1.call-start = ((), (), s32[]{:S(2)}) async-start(), calls=%async_computation.1 | async-start | bytes 8515584 | tf_op jit(solution)/shard_map/all_gather | solution.py:53
  8.4 198.6 %all-gather.6.cloned.1.call-start = ((), (), s32[]{:S(2)}) async-start(), calls=%async_computation | async-start | bytes 4325376 | tf_op jit(solution)/shard_map/all_gather | solution.py:75
  8.5 43.0 %collective-permute-start = (bf16[256,3584]{1,0:T(8,128)(2,1)}, bf16[256,3584]{1,0:T(8,128)(2,1)S(1)}, u32[]{:S(2)}, u32[]{:S(2)}) collective-permute-start(bf16[256,3584]{1,0:T(8,128)(2,1)} %bitcast.20), channel_id=1, source_target_pairs={{0,64},{64,128},{128,192},{1,65},{65,129},{129,193},{2,66},{66,130... | collective-permute-start | bytes 5505032 | tf_op jit(solution)/shard_map/ppermute | solution.py:15
  51.5 70.6 %copy-start.2 = (bf16[256,3584]{1,0:T(8,128)(2,1)}, bf16[256,3584]{1,0:T(8,128)(2,1)S(1)}, u32[]{:S(2)}) copy-start(bf16[256,3584]{1,0:T(8,128)(2,1)S(1)} %collective-permute-done) | copy-start | bytes 5505028
  51.9 76.2 %copy-start.5 = (s32[2]{0:T(128)S(1)}, s32[2]{0:T(128)}, u32[]{:S(2)}) copy-start(s32[2]{0:T(128)} %param.20) | copy-start | bytes 28
  123.6 177.4 %all-gather.10.cloned.1.call-start = ((), (), s32[]{:S(2)}) async-start(), calls=%async_computation.2 | async-start | bytes 6623232 | tf_op jit(solution)/shard_map/all_gather | solution.py:105
  254.3 46.8 %copy-start.3 = (bf16[128,1024]{1,0:T(8,128)(2,1)S(1)}, bf16[128,1024]{1,0:T(8,128)(2,1)}, u32[]{:S(2)}) copy-start(bf16[128,1024]{1,0:T(8,128)(2,1)} %param.19) | copy-start | bytes 786436
  254.3 46.7 %copy-start.6 = (f32[1024]{0:T(1024)S(1)}, f32[1024]{0:T(1024)}, u32[]{:S(2)}) copy-start(f32[1024]{0:T(1024)} %param.21) | copy-start | bytes 12292
  307.2 48.8 %copy-start.4 = (f32[3584]{0:T(1024)S(1)}, f32[3584]{0:T(1024)}, u32[]{:S(2)}) copy-start(f32[3584]{0:T(1024)} %param.23) | copy-start | bytes 43012
  314.5 46.7 %copy-start.1 = (bf16[3,112,1152]{2,1,0:T(8,128)(2,1)S(1)}, bf16[3,112,1152]{2,1,0:T(8,128)(2,1)}, u32[]{:S(2)}) copy-start(bf16[3,112,1152]{2,1,0:T(8,128)(2,1)} %param.25) | copy-start | bytes 2322436
  314.5 41.6 %collective-permute-start.1 = (bf16[256,3584]{1,0:T(8,128)(2,1)}, bf16[256,3584]{1,0:T(8,128)(2,1)S(1)}, u32[]{:S(2)}, u32[]{:S(2)}) collective-permute-start(bf16[256,3584]{1,0:T(8,128)(2,1)} %get-tuple-element.107), channel_id=1, source_target_pairs={{0,1},{1,0},{2,3},{3,2},{4,5},{5,4},{6,7},{7,6},{8,9},{9,8},{10,11... | collective-permute-start | bytes 5505032 | tf_op jit(solution)/shard_map/ppermute | solution.py:136
Sparse Core Ops, SparseCore 0:
  10.0 105.1 all-gather.7
  123.7 83.2 all-gather.5
  209.7 91.2 all-gather.9
where the time goes:
time: 369 us; the launch traced here: 368 us
  waiting for transfers between devices  223 us (60%)
  matrix products  69.9 us (19%)
  other arithmetic  39.4 us (11%)
  local copies, waits for them, and re-layouts  15.9 us (4%)
  between operations  14.5 us (4%)
  starting transfers between devices  4.56 us (1%)
    all_gather x1, waiting for transfers between devices, on_device(): lax.all_gather(merged[:, query_cols:query_cols + 2 * HD], 'ctx', axis=0,...  78.7 us
    all_gather x1, waiting for transfers between devices, on_device(): lax.all_gather(weight_qkv, 'ctx', axis=0, tiled=True)  63.3 us
    ppermute x1, waiting for transfers between devices, on_device(): other_term = lax.ppermute(own_term, 'tp', [(0, 1), (1, 0)])  41.2 us
    ppermute x1, waiting for transfers between devices, shifted(): return lax.ppermute(value, axis, pairs)  37.2 us
    reduce_sum x2, other arithmetic, update_state(): total_new = jnp.sum(weights, axis=1)  29.2 us
    dot_general x2, matrix products, update_state(): jnp.dot(query_flat, keys_in.T, preferred_element_type=jnp.float32)  28 us
    dot_general x2, matrix products, update_state(): jnp.dot(weights.astype(jnp.bfloat16), values_in, preferred_element_type=j...  26.2 us
  transfers between devices with their start and end apart: 5, of which 5 were waited for; matrix products, arithmetic and copies ran while one was open for 26% of the time, Pallas kernels for 0%

commit v1 on v0

--- a/solution.py
+++ b/solution.py
@@ -48,11 +48,16 @@
     normed = (
         inputs * lax.rsqrt(jnp.mean(inputs * inputs, axis=1, keepdims=True) + 1e-06) * layer_gain
     ).astype(jnp.bfloat16)
-    merged = jnp.dot(
-        normed,
-        lax.all_gather(weight_qkv, "ctx", axis=0, tiled=True),
-        preferred_element_type=jnp.float32,
+    draw_space = lambda v0: jnp.concatenate(
+        lax.all_to_all(
+            jnp.stack([v0 for _ in range(lax.axis_size("ctx"))]),
+            axis_name="ctx",
+            split_axis=0,
+            concat_axis=0,
+        ),
+        axis=0,
     )
+    merged = jnp.dot(normed, draw_space(weight_qkv), preferred_element_type=jnp.float32)
     merged = (merged + bias_qkv).astype(jnp.bfloat16)
     query_cols = GROUP * HD
     queries = merged[:, :query_cols]

time: 369 us -> 466 us (1.26)
  waiting for transfers between devices: 223 us -> 305 us
  starting transfers between devices: 4.56 us -> 16.3 us
    all_to_all x0 -> x1, waiting for transfers between devices: none -> 140 us  [on_device(): lax.all_to_all(jnp.stack([v0 for _ in range(lax.axis_size('ctx'))]), axis...]
    all_gather x1 -> x0, waiting for transfers between devices: 63.3 us -> none  [on_device(): lax.all_gather(weight_qkv, 'ctx', axis=0, tiled=True)]
    all_to_all x0 -> x1, starting transfers between devices: none -> 12.6 us  [on_device(): lax.all_to_all(jnp.stack([v0 for _ in range(lax.axis_size('ctx'))]), axis...]
    all_gather x1, waiting for transfers between devices: 78.7 us -> 84.1 us  [on_device(): lax.all_gather(merged[:, query_cols:query_cols + 2 * HD], 'ctx', axis=0,...]
  transfers between devices with their start and end apart: 5 -> 5, of which waited for: 5 -> 5; matrix products, arithmetic and copies ran while one was open for 26% -> 21% of each run, Pallas kernels for 0% -> 0%
where the time goes in v1:
time: 466 us; the launch traced here: 465 us
  waiting for transfers between devices  305 us (65%)
  matrix products  69.7 us (15%)
  other arithmetic  39.4 us (8%)
  local copies, waits for them, and re-layouts  18.9 us (4%)
  starting transfers between devices  16.3 us (3%)
  between operations  14.8 us (3%)
    all_to_all x1, waiting for transfers between devices, on_device(): lax.all_to_all(jnp.stack([v0 for _ in range(lax.axis_size('ctx'))]), axis...  140 us
    all_gather x1, waiting for transfers between devices, on_device(): lax.all_gather(merged[:, query_cols:query_cols + 2 * HD], 'ctx', axis=0,...  84.1 us
    ppermute x1, waiting for transfers between devices, on_device(): other_term = lax.ppermute(own_term, 'tp', [(0, 1), (1, 0)])  41.3 us
    ppermute x1, waiting for transfers between devices, shifted(): return lax.ppermute(value, axis, pairs)  37.7 us
    reduce_sum x2, other arithmetic, update_state(): total_new = jnp.sum(weights, axis=1)  29.2 us
    dot_general x2, matrix products, update_state(): jnp.dot(query_flat, keys_in.T, preferred_element_type=jnp.float32)  27.8 us
    dot_general x2, matrix products, update_state(): jnp.dot(weights.astype(jnp.bfloat16), values_in, preferred_element_type=j...  26.2 us
    all_to_all x1, starting transfers between devices, on_device(): lax.all_to_all(jnp.stack([v0 for _ in range(lax.axis_size('ctx'))]), axis...  12.6 us
  transfers between devices with their start and end apart: 5, of which 5 were waited for; matrix products, arithmetic and copies ran while one was open for 21% of the time, Pallas kernels for 0%

profile of v1, /device:TPU:1, one launch (start us, length us, event | category | flops | bytes accessed | tf_op | source)
XLA Modules:
  0.0 465.0 jit_solution(17341451175194634249)
XLA Ops:
  6.5 1.1 copy-done
  7.7 3.8 stack.2
  11.5 12.6 %all-to-all-start = ((bf16[32,112,1152]{2,1,0:T(8,128)(2,1)}), bf16[32,112,1152]{2,1,0:T(8,128)(2,1)}, u32[]{:S(2)}, u32[]{:S(2)}) async-start(bf16[32,112,1152]{2,1,0:T(8,128)(2,1)} %stack.2), calls=%async_computation | async-start | bytes 16515072 | tf_op jit(solution)/shard_map/all_to_all | solution.py:52
  24.2 3.3 collective-permute-start
  27.5 0.7 dynamic-slice_reduce_fusion.1
  28.2 0.9 dynamic-slice_reduce_fusion
  29.1 37.7 %collective-permute-done = bf16[256,3584]{1,0:T(8,128)(2,1)S(1)} collective-permute-done((bf16[256,3584]{1,0:T(8,128)(2,1)}, bf16[256,3584]{1,0:T(8,128)(2,1)S(1)}, u32[]{:S(2)}, u32[]{:S(2)}) %collective-permute-start) | collective-permute-done | bytes 1835040 | tf_op jit(solution)/shard_map/ppermute | solution.py:15
  66.8 0.4 fusion.29
  67.2 139.7 %all-to-all-done = bf16[32,112,1152]{2,1,0:T(8,128)(2,1)} async-done(((bf16[32,112,1152]{2,1,0:T(8,128)(2,1)}), bf16[32,112,1152]{2,1,0:T(8,128)(2,1)}, u32[]{:S(2)}, u32[]{:S(2)}) %all-to-all-start) | async-done | bytes 8257568 | tf_op jit(solution)/shard_map/all_to_all | solution.py:52
  206.9 6.8 %fusion.32 = bf16[256,1152]{1,0:T(8,128)(2,1)} fusion(bf16[3584,1152]{1,0:T(8,128)(2,1)} %bitcast.2, bf16[256,3584]{1,0:T(8,128)(2,1)S(1)} %collective-permute-done, f32[3584]{0:T(1024)S(1)} %dynamic-slice_reduce_fusion, f32[256]{0:T(256)S(1)} %add_rsqrt_fusion.1, f32[1152]{0:T(1024)S(1)} %dynamic-slice_reduce_fusion.1), kind=kOutput, calls=%fused_computation.54 | convolution fusion | flops 2118189056 | bytes 10702336 | tf_op jit(solution)/shard_map/dot_general | solution.py:60
  213.7 1.6 slice.25
  215.3 1.6 constant_dynamic-slice_fusion
  217.0 0.7 broadcast_reduce_fusion.1
  218.4 0.7 broadcast_reduce_fusion
  219.8 0.1 fusion.41
  220.0 84.1 %all-gather.4.cloned.1.call-done = bf16[8192,256]{1,0:T(8,128)(2,1)} async-done(((bf16[256,256]{1,0:T(8,128)(2,1)}), bf16[8192,256]{1,0:T(8,128)(2,1)}) %all-gather.4.cloned.1.call-update) | async-done | bytes 4194320 | tf_op jit(solution)/shard_map/all_gather | solution.py:80
  304.1 3.9 fusion.42
  308.0 42.9 %conditional.3 = (f32[896]{0:T(1024)S(1)}, f32[896,128]{1,0:T(8,128)S(1)}) conditional(s32[]{:T(128)} %convert_element_type.60, () %tuple.37, (s32[128,7]{1,0:T(8,128)S(1)}, bf16[256,1152]{1,0:T(8,128)(2,1)}, bf16[8192,128]{1,0:T(8,128)(2,1)}, bf16[8192,128]{1,0:T(8,128)(2,1)S(1)}) %tuple.38), branch_computations={%region_3.4_spmd, %region_4.7_spmd} | conditional | flops 3875535872 | bytes 93919760 | solution.py:96
  308.2 0.2 le.30
  308.4 1.0 slice.15
  309.4 0.2 reshape.66
  309.6 13.8 %fusion = (f32[896]{0:T(1024)S(1)}, f32[896,8192]{1,0:T(8,128)}) fusion(s32[896]{0:T(1024)S(1)} %le.30, bf16[896,128]{1,0:T(8,128)(2,1)S(1)} %reshape.66, bf16[8192,128]{1,0:T(8,128)(2,1)} %get-tuple-element.49), kind=kOutput, calls=%fused_computation.4 | convolution fusion | flops 1908407424 | bytes 31693824 | tf_op jit(solution)/shard_map/cond/branch_1_fun/dot_general | solution.py:21
  323.5 13.1 %fusion.3 = f32[896,128]{1,0:T(8,128)S(1)} fusion(bf16[8192,128]{1,0:T(8,128)(2,1)S(1)} %get-tuple-element.50, f32[896,8192]{1,0:T(8,128)} %get-tuple-element.92, f32[896]{0:T(1024)S(1)} %broadcast_maximum_fusion, s32[896]{0:T(1024)S(1)} %le.30), kind=kOutput, calls=%fused_computation.7 | convolution fusion | flops 1923088384 | bytes 31923200 | tf_op jit(solution)/shard_map/cond/branch_1_fun/dot_general | solution.py:27
  336.5 14.4 %fusion.2 = f32[896]{0:T(1024)S(1)} fusion(f32[896,8192]{1,0:T(8,128)} %get-tuple-element.92, f32[896]{0:T(1024)S(1)} %broadcast_maximum_fusion, s32[896]{0:T(1024)S(1)} %le.30), kind=kLoop, calls=%fused_computation.6 | loop fusion | flops 44039296 | bytes 29370880 | tf_op jit(solution)/shard_map/cond/branch_1_fun/reduce_sum | solution.py:26
  351.0 0.2 divide_convert_fusion.1
  351.2 0.2 reshape.72
  351.4 0.1 broadcast_in_dim.105
  351.5 43.5 %conditional.4 = (f32[896]{0:T(1024)S(1)}, f32[896,128]{1,0:T(8,128)S(1)}) conditional(s32[]{:T(128)} %convert_element_type.64, () %tuple.39, (s32[128,7]{1,0:T(8,128)S(1)}, bf16[256,1152]{1,0:T(8,128)(2,1)}, bf16[8192,128]{1,0:T(8,128)(2,1)}, bf16[8192,128]{1,0:T(8,128)(2,1)S(1)}) %tuple.40), branch_computations={%region_8.9_spmd, %region_9.12_spmd} | conditional | flops 3875535872 | bytes 93919760 | solution.py:96
  351.8 0.2 le.38
  352.0 1.0 slice.16
  352.9 0.2 reshape.67
  353.2 14.0 %fusion.8 = (f32[896]{0:T(1024)S(1)}, f32[896,8192]{1,0:T(8,128)}) fusion(s32[896]{0:T(1024)S(1)} %le.38, bf16[896,128]{1,0:T(8,128)(2,1)S(1)} %reshape.67, bf16[8192,128]{1,0:T(8,128)(2,1)} %get-tuple-element.53), kind=kOutput, calls=%fused_computation.15 | convolution fusion | flops 1908407424 | bytes 31693824 | tf_op jit(solution)/shard_map/cond/branch_1_fun/dot_general | solution.py:21
  367.2 13.1 %fusion.11 = f32[896,128]{1,0:T(8,128)S(1)} fusion(bf16[8192,128]{1,0:T(8,128)(2,1)S(1)} %get-tuple-element.54, f32[896,8192]{1,0:T(8,128)} %get-tuple-element.94, f32[896]{0:T(1024)S(1)} %broadcast_maximum_fusion.1, s32[896]{0:T(1024)S(1)} %le.38), kind=kOutput, calls=%fused_computation.18 | convolution fusion | flops 1923088384 | bytes 31923200 | tf_op jit(solution)/shard_map/cond/branch_1_fun/dot_general | solution.py:27
  380.3 14.8 %fusion.10 = f32[896]{0:T(1024)S(1)} fusion(f32[896,8192]{1,0:T(8,128)} %get-tuple-element.94, f32[896]{0:T(1024)S(1)} %broadcast_maximum_fusion.1, s32[896]{0:T(1024)S(1)} %le.38), kind=kLoop, calls=%fused_computation.17 | loop fusion | flops 44039296 | bytes 29370880 | tf_op jit(solution)/shard_map/cond/branch_1_fun/reduce_sum | solution.py:26
  395.1 0.2 divide_convert_fusion
  395.3 0.2 reshape.73
  395.5 2.5 all-gather.6.cloned.1.call-done
  398.1 6.2 %fusion.25 = bf16[256,3584]{1,0:T(8,128)(2,1)} fusion(bf16[1,896,3584]{1,2,0:T(8,128)(2,1)} %all-gather.6.cloned.1.call-done, bf16[128,896]{1,0:T(8,128)(2,1)S(1)} %reshape.73, bf16[128,896]{1,0:T(8,128)(2,1)S(1)} %reshape.72), kind=kOutput, calls=%fused_computation.43 | convolution fusion | flops 1645084672 | bytes 8716288 | tf_op jit(solution)/shard_map/dot_general | solution.py:108
  404.2 7.3 %conditional.5 = (bf16[256,3584]{1,0:T(8,128)(2,1)}) conditional(s32[]{:T(128)} %convert_element_type.59, bf16[256,3584]{1,0:T(8,128)(2,1)} %fusion.25, (pred[256]{0:T(512)(128)(4,1)S(1)}, pred[256,2]{0,1:T(4,128)(4,1)S(1)}, bf16[128,1024]{1,0:T(8,128)(2,1)S(1)}, f32[1024]{0:T(1024)S(1)}, s32[]{:T(128)}, /*index=5*/bf16[512,3584]{1,0:T(8,128)(2,1)}, ...), branch_computations={%region_13.14_spmd, %region_14.17_spmd} | conditional | flops 472585344 | bytes 13264226 | solution.py:136
  404.3 0.1 convert_reduce_fusion
  404.4 0.2 multiply_reduce_fusion
  404.7 2.7 fusion.18
  407.4 0.1 fusion.23
  407.5 1.7 gather_fusion
  409.3 2.2 select_select_fusion
  411.5 0.3 collective-permute-start.1
  411.8 41.3 %collective-permute-done.1 = bf16[256,3584]{1,0:T(8,128)(2,1)S(1)} collective-permute-done((bf16[256,3584]{1,0:T(8,128)(2,1)}, bf16[256,3584]{1,0:T(8,128)(2,1)S(1)}, u32[]{:S(2)}, u32[]{:S(2)}) %collective-permute-start.1) | collective-permute-done | bytes 1835040 | tf_op jit(solution)/shard_map/ppermute | solution.py:141
  453.1 5.1 %fusion.34 = bf16[1,256,3584]{2,1,0:T(8,128)(2,1)} fusion(bf16[256,3584]{1,0:T(8,128)(2,1)S(1)} %collective-permute-done.1, bf16[256,3584]{1,0:T(8,128)(2,1)} %get-tuple-element.107, bf16[256,3584]{1,0:T(8,128)(2,1)} %copy-done.2, bf16[256,3584]{1,0:T(8,128)(2,1)} %param.18, f32[3584]{0:T(1024)S(1)} %copy-done.4, pred[256]{0:T(512)(128)(4,1)S(1)} %get-tuple-element.89, ...), kind=kLoop, calls=%fused_computation.55 | loop fusion | flops 8257536 | bytes 9189633 | tf_op jit(solution)/shard_map/broadcast_in_dim | solution.py:144
  (36 shorter events, 0.5 us)
Async XLA Ops:
  6.5 1.1 copy-start
  11.5 195.4 %all-to-all-start = ((bf16[32,112,1152]{2,1,0:T(8,128)(2,1)}), bf16[32,112,1152]{2,1,0:T(8,128)(2,1)}, u32[]{:S(2)}, u32[]{:S(2)}) async-start(bf16[32,112,1152]{2,1,0:T(8,128)(2,1)} %stack.2), calls=%async_computation | async-start | bytes 16515072 | tf_op jit(solution)/shard_map/all_to_all | solution.py:52
  24.1 280.0 %all-gather.4.cloned.1.call-start = ((), (), s32[]{:S(2)}) async-start(), calls=%async_computation.1 | async-start | bytes 4325376 | tf_op jit(solution)/shard_map/all_gather | solution.py:80
  24.2 42.6 %collective-permute-start = (bf16[256,3584]{1,0:T(8,128)(2,1)}, bf16[256,3584]{1,0:T(8,128)(2,1)S(1)}, u32[]{:S(2)}, u32[]{:S(2)}) collective-permute-start(bf16[256,3584]{1,0:T(8,128)(2,1)} %bitcast.17), channel_id=1, source_target_pairs={{0,64},{64,128},{128,192},{1,65},{65,129},{129,193},{2,66},{66,130... | collective-permute-start | bytes 5505032 | tf_op jit(solution)/shard_map/ppermute | solution.py:15
  66.8 146.9 %copy-start.2 = (bf16[256,3584]{1,0:T(8,128)(2,1)}, bf16[256,3584]{1,0:T(8,128)(2,1)S(1)}, u32[]{:S(2)}) copy-start(bf16[256,3584]{1,0:T(8,128)(2,1)S(1)} %collective-permute-done) | copy-start | bytes 5505028
  206.9 12.9 %copy-start.5 = (s32[2]{0:T(128)S(1)}, s32[2]{0:T(128)}, u32[]{:S(2)}) copy-start(s32[2]{0:T(128)} %param.20) | copy-start | bytes 28
  215.3 182.8 %all-gather.6.cloned.1.call-start = ((), (), s32[]{:S(2)}) async-start(), calls=%async_computation.2 | async-start | bytes 6623232 | tf_op jit(solution)/shard_map/all_gather | solution.py:110
  351.5 46.5 %copy-start.3 = (bf16[128,1024]{1,0:T(8,128)(2,1)S(1)}, bf16[128,1024]{1,0:T(8,128)(2,1)}, u32[]{:S(2)}) copy-start(bf16[128,1024]{1,0:T(8,128)(2,1)} %param.19) | copy-start | bytes 786436
  351.5 46.5 %copy-start.6 = (f32[1024]{0:T(1024)S(1)}, f32[1024]{0:T(1024)}, u32[]{:S(2)}) copy-start(f32[1024]{0:T(1024)} %param.21) | copy-start | bytes 12292
  404.2 48.8 %copy-start.4 = (f32[3584]{0:T(1024)S(1)}, f32[3584]{0:T(1024)}, u32[]{:S(2)}) copy-start(f32[3584]{0:T(1024)} %param.23) | copy-start | bytes 43012
  411.5 46.7 %copy-start.1 = (bf16[3,112,1152]{2,1,0:T(8,128)(2,1)S(1)}, bf16[3,112,1152]{2,1,0:T(8,128)(2,1)}, u32[]{:S(2)}) copy-start(bf16[3,112,1152]{2,1,0:T(8,128)(2,1)} %param.25) | copy-start | bytes 2322436
  411.5 41.6 %collective-permute-start.1 = (bf16[256,3584]{1,0:T(8,128)(2,1)}, bf16[256,3584]{1,0:T(8,128)(2,1)S(1)}, u32[]{:S(2)}, u32[]{:S(2)}) collective-permute-start(bf16[256,3584]{1,0:T(8,128)(2,1)} %get-tuple-element.107), channel_id=1, source_target_pairs={{0,1},{1,0},{2,3},{3,2},{4,5},{5,4},{6,7},{7,6},{8,9},{9,8},{10,11... | collective-permute-start | bytes 5505032 | tf_op jit(solution)/shard_map/ppermute | solution.py:141
Sparse Core Ops, SparseCore 0:
  215.4 88.6 all-gather.3
  306.8 91.2 all-gather.5
